TPU v7x, 32 devices: a whole 2x2x4 slice. The times are simulated.
32 devices in a mesh: groups: 2 (over y), ctx: 4 (over z), head: 2 (over x), rep: 2 (over core).
Axes of the slice: x: 2, y: 2, z: 4, core: 2. Of those that a mesh axis runs over, the one named last changes fastest.
Arguments:
- query: bfloat16 [2048, 4096], P(('groups', 'ctx', 'rep'), 'head'), parts along dimension 0, may hold values from -23.069359 to 23.069359
- key: bfloat16 [4096, 1024], P(('groups', 'ctx'), 'head'), parts along dimension 0, may hold values from -6 to 6
- value: bfloat16 [4096, 1024], P(('groups', 'ctx'), 'head'), parts along dimension 0, may hold values from -24 to 24
- out_weight: bfloat16 [4096, 4096], P('head'), may hold values from -0.375 to 0.375
- cotangent: bfloat16 [2048, 4096], P(('groups', 'ctx', 'rep')), parts along dimension 0, may hold values from -6 to 6
- response: int32 [2048], P(('groups', 'ctx', 'rep')), parts along dimension 0, may hold values 0 or 1
- segment_ids: int32 [4096], P(('groups', 'ctx')), parts along dimension 0, may hold values from 0 to 31, never falling along the last dimension, each value on 1 to 128 neighbouring positions
- masked_segments: int32 [8], P('groups'), parts along dimension 0, may hold values from 0 to 31
Outputs:
- patch_effect: bfloat16 [2048, 4096], P(('groups', 'ctx', 'rep'), 'head'), parts along dimension 0
- token_attr: float32 [4096], P(('groups', 'ctx')), parts along dimension 0
- segment_attr: float32 [64], P('groups'), parts along dimension 0
There are 2 independent parts, one for each index of `groups`. A program takes and returns all parts, laid end to end along the dimension named above; an argument that names none is the same for every part. Nothing has to cross between parts.
All inputs are finite; a program needn't handle non-finite values. No bound on the sum of `response` on one device may be relied on, other than what follows from the above.
Results may differ from a plain program's by a relative error of at most 0.0095.
Values may be sent and summed in bfloat16 or wider, within the bound.
No kernel may reach another device: no remote copies, remote signals or barrier semaphores. Data moves between devices by JAX's collectives and lax.ppermute only.
A program may use at most 128 MiB of HBM per device.

v0:
```python
from functools import partial
import jax
import jax.numpy as jnp
from jax import lax
from jax.sharding import PartitionSpec as P

HD = 128
SEG_DEV = 8
NEG_FILL = -1e30


def split_heads(incoming):
    return incoming.reshape(incoming.shape[0], -1, HD)


def block_scores(query_rows, key_block):
    raw_scores = jnp.einsum(
        "gqd,tgd->gqt", query_rows, split_heads(key_block), preferred_element_type=jnp.float32
    )
    return raw_scores * HD ** (-0.5)


def visible_keys(row_pos, first_key, key_rows):
    key_pos = first_key + jnp.arange(key_rows, dtype=jnp.int32)
    return key_pos[None, None, :] <= row_pos[None, :, None]


def online_update(running, scores, allowed, value_heads):
    row_top, row_total, weighted = running
    chosen = jnp.where(allowed, scores, NEG_FILL)
    new_top = jnp.maximum(row_top, jnp.max(chosen, axis=2))
    shrink = jnp.exp(row_top - new_top)
    weights = jnp.where(allowed, jnp.exp(chosen - new_top[:, :, None]), 0.0)
    row_total = row_total * shrink + jnp.sum(weights, axis=2)
    weighted = weighted * shrink[:, :, None] + jnp.einsum(
        "gqt,tgd->gqd",
        weights.astype(jnp.bfloat16),
        value_heads,
        preferred_element_type=jnp.float32,
    )
    return (new_top, row_total, weighted)


def forward_piece(query_rows, row_pos, running, incoming, first_key):
    key_block, value_block, kept_flag = incoming
    scores = block_scores(query_rows, key_block)
    visible = visible_keys(row_pos, first_key, key_block.shape[0])
    kept_visible = jnp.logical_and(visible, kept_flag[None, None, :] > 0)
    value_heads = split_heads(value_block)
    return (
        online_update(running[0], scores, visible, value_heads),
        online_update(running[1], scores, kept_visible, value_heads),
    )


def backward_terms(
    query_rows, row_pos, grad_rows, log_total, row_dot, key_block, value_block, first_key
):
    scores = block_scores(query_rows, key_block)
    visible = visible_keys(row_pos, first_key, key_block.shape[0])
    shifted = jnp.where(visible, scores - log_total[:, :, None], 0.0)
    probability = jnp.where(visible, jnp.exp(shifted), 0.0)
    grad_prob = jnp.einsum(
        "gqd,tgd->gqt", grad_rows, split_heads(value_block), preferred_element_type=jnp.float32
    )
    return jnp.sum(
        probability * (grad_prob + (grad_prob - row_dot[:, :, None]) * shifted), axis=(0, 1)
    )


def blockwise(stepper, state_in, incoming, block_rows):
    length = jax.tree.leaves(incoming)[0].shape[0]

    def advance(counter, state_now):
        offset = counter * block_rows
        portion = jax.tree.map(
            lambda member: lax.dynamic_slice_in_dim(member, offset, block_rows, 0), incoming
        )
        return stepper(state_now, portion, offset)

    return lax.fori_loop(0, length // block_rows, advance, state_in)


def finish_pass(running):
    row_top, row_total, weighted = running
    return (weighted / row_total[:, :, None], row_top + jnp.log(row_total))


def local(query, key, value, out_weight, cotangent, response, segment_ids, masked_segments):
    ctx_count = lax.axis_size("ctx")
    rep_count = lax.axis_size("rep")
    ctx_at = lax.axis_index("ctx")
    rep_at = lax.axis_index("rep")
    query_count = query.shape[0]
    key_count = key.shape[0]
    kv_local = key.shape[1] // HD
    heads_local = query.shape[1] // HD
    group_size = heads_local // kv_local
    context_len = key_count * ctx_count
    query_base = context_len - query_count * ctx_count * rep_count
    row_width = group_size * query_count
    kept_flag = jnp.where(
        jnp.any(segment_ids[:, None] == masked_segments[None, :], axis=1), 0.0, 1.0
    ).astype(jnp.bfloat16)
    grad_masked = jnp.where(response[:, None] > 0, cotangent, jnp.zeros_like(cotangent))
    grad_out = jnp.dot(grad_masked, out_weight.T, preferred_element_type=jnp.float32).astype(
        jnp.bfloat16
    )

    def grouped(rows_in):
        return rows_in.reshape(query_count, kv_local, group_size, HD).transpose(1, 2, 0, 3)

    fresh_state = (
        jnp.full((kv_local, row_width), NEG_FILL, jnp.float32),
        jnp.zeros((kv_local, row_width), jnp.float32),
        jnp.zeros((kv_local, row_width, HD), jnp.float32),
    )
    starting = (fresh_state, fresh_state)
    query_rows = grouped(query).reshape(kv_local, row_width, HD)
    grad_own = grouped(grad_out).reshape(kv_local, row_width, HD)
    base_pos = (
        query_base
        + (ctx_at * rep_count + rep_at) * query_count
        + jnp.arange(query_count, dtype=jnp.int32)
    )
    own_pos = jnp.tile(base_pos, group_size)
    forward_step = partial(forward_piece, query_rows, own_pos)
    running = blockwise(
        forward_step,
        starting,
        (
            lax.all_gather(key, "ctx", axis=0, tiled=True),
            lax.all_gather(value, "ctx", axis=0, tiled=True),
            lax.all_gather(kept_flag, "ctx", axis=0, tiled=True),
        ),
        key_count,
    )
    clean_out, log_total = finish_pass(running[0])
    masked_out, _ = finish_pass(running[1])
    row_dot = jnp.sum(grad_own.astype(jnp.float32) * clean_out, axis=2)

    def backward_step(total_now, incoming, first_key):
        added = backward_terms(
            query_rows, own_pos, grad_own, log_total, row_dot, incoming[0], incoming[1], first_key
        )
        current = lax.dynamic_slice_in_dim(total_now, first_key, incoming[0].shape[0], 0)
        return lax.dynamic_update_slice_in_dim(total_now, current + added, first_key, 0)

    empty_attr = jnp.zeros((context_len,), jnp.float32)
    attr_all = blockwise(
        backward_step,
        empty_attr,
        (
            lax.all_gather(key, "ctx", axis=0, tiled=True),
            lax.all_gather(value, "ctx", axis=0, tiled=True),
        ),
        key_count,
    )
    local_attr = lax.psum_scatter(attr_all, "ctx", scatter_dimension=0, tiled=True)
    change = (
        (masked_out - clean_out)
        .reshape(kv_local, group_size, query_count, HD)
        .transpose(2, 0, 1, 3)
        .reshape(query_count, heads_local * HD)
        .astype(jnp.bfloat16)
    )
    projected = jnp.dot(change, out_weight, preferred_element_type=jnp.float32)
    patch_effect = lax.psum_scatter(projected, "head", scatter_dimension=1, tiled=True).astype(
        jnp.bfloat16
    )
    token_attr = lax.psum(local_attr, ("head", "rep"))
    onehot = (
        segment_ids[:, None] == jnp.arange(SEG_DEV * ctx_count, dtype=jnp.int32)[None, :]
    ).astype(jnp.float32)
    segment_attr = lax.psum(jnp.dot(token_attr, onehot, precision=lax.Precision.HIGHEST), "ctx")
    return (patch_effect, token_attr, segment_attr)


def solution(mesh):
    return jax.shard_map(
        local,
        mesh=mesh,
        in_specs=(
            P(("groups", "ctx", "rep"), "head"),
            P(("groups", "ctx"), "head"),
            P(("groups", "ctx"), "head"),
            P("head", None),
            P(("groups", "ctx", "rep"), None),
            P(("groups", "ctx", "rep")),
            P(("groups", "ctx")),
            P("groups"),
        ),
        out_specs=(P(("groups", "ctx", "rep"), "head"), P(("groups", "ctx")), P("groups")),
        check_vma=False,
    )
```

profile of v0, /device:TPU:0, one launch (start us, length us, event | category | flops | bytes accessed | tf_op | source)
XLA Modules:
  0.0 224.0 jit_solution(5980120812336782876)
XLA Ops:
  7.3 2.1 copy.57
  9.5 2.0 copy.59
  13.3 13.7 %all-gather = bf16[4,1,512]{2,1,0:T(2,128)(2,1)S(1)} all-gather(bf16[1,1,512]{2,1,0:T(2,128)(2,1)S(1)} %reshape.205), channel_id=1, replica_groups=mesh['groups'=2,'ctx'=4,'head'=2,'rep'=2] {'ctx'}, dimensions={0}, use_global_device_ids=true | all-gather | bytes 5120 | tf_op jit(solution)/shard_map/all_gather | solution.py:134
  27.1 11.5 %convolution_convert_fusion = bf16[128,2048]{1,0:T(8,128)(2,1)S(1)} fusion(bf16[2048,4096]{1,0:T(8,128)(2,1)} %param.15, bf16[128,4096]{1,0:T(8,128)(2,1)S(1)} %copy-done.3, pred[128]{0:T(512)(128)(4,1)S(1)} %broadcast_compare_fusion.2), kind=kOutput, calls=%fused_computation.53 | convolution fusion | flops 2148270080 | bytes 18350208 | tf_op jit(solution)/shard_map/dot_general | solution.py:106
  40.5 18.3 %all-gather.4.cloned.1.call-done = bf16[2048,512]{0,1:T(8,128)(2,1)} async-done(((bf16[512,512]{0,1:T(8,128)(2,1)}), bf16[2048,512]{0,1:T(8,128)(2,1)}) %all-gather.4.cloned.1.call-update) | async-done | bytes 2097168 | tf_op jit(solution)/shard_map/all_gather | solution.py:132
  58.9 46.4 %all-gather.6.cloned.1.call-done = bf16[2048,512]{0,1:T(8,128)(2,1)} async-done(((bf16[512,512]{0,1:T(8,128)(2,1)}), bf16[2048,512]{0,1:T(8,128)(2,1)}) %all-gather.6.cloned.1.call-update) | async-done | bytes 2097168 | tf_op jit(solution)/shard_map/all_gather | solution.py:133
  105.2 54.5 %while.39 = (s32[]{:T(128)}, f32[4,512]{1,0:T(4,128)S(1)}, f32[4,512]{1,0:T(4,128)S(1)}, f32[4,512,128]{2,1,0:T(8,128)S(1)}, f32[4,512]{1,0:T(4,128)S(1)}, /*ind...) while((s32[]{:T(128)}, f32[4,512]{1,0:T(4,128)S(1)}, ...), condition=%wide.region_6.7_spmd.clone, body=%wide.region_1.6_spmd.clone.sunk | while | flops 832591872 | bytes 52702004 | solution.py:81
  106.7 3.4 %fusion.81 = (f32[4,512]{1,0:T(4,128)S(1)}, f32[4,512]{1,0:T(4,128)S(1)}, f32[4,512,512]{2,1,0:T(8,128)}) fusion(pred[512,512]{0,1:T(8,128)(4,1)S(1)} %get-tuple-element.631, pred[512,512]{0,1:T(8,128)(4,1)S(1)} %get-tuple-element.632, bf16[512,4,128]{0,2,1:T(8,128)(2,1)S(1)} %bitcast.121, bf16[4,512,128]{2,1,0:T(8,128)(2,1)S(1)} %get-tuple-element.682), kind=kOutput, calls=%fused_computation.19.clone.1 | convolution fusion | flops 273674240 | bytes 5783552 | tf_op jit(solution)/shard_map/while/body/eval_jaxpr/gqd,tgd->gqt/dot_general | solution.py:17
  110.1 3.7 %fusion.82 = (f32[4,512]{1,0:T(4,128)S(1)}, f32[4,512]{1,0:T(4,128)S(1)}) fusion(f32[4,512,512]{2,1,0:T(8,128)} %get-tuple-element.634, f32[4,512]{1,0:T(4,128)S(1)} %select_maximum_fusion.5, pred[512,512]{0,1:T(8,128)(4,1)S(1)} %get-tuple-element.631, f32[4,512]{1,0:T(4,128)S(1)} %select_maximum_fusion.4, pred[512,512]{0,1:T(8,128)(4,1)S(1)} %get-tuple-element.632), kind=kLoop, calls=%fused_computation.23.clone.1 | loop fusion | flops 9433088 | bytes 4751360 | tf_op jit(solution)/shard_map/while/body/eval_jaxpr/reduce_sum | solution.py:34
  115.0 1.9 fusion.85
  116.9 1.9 fusion.84
  120.4 3.4 %fusion.81 = (f32[4,512]{1,0:T(4,128)S(1)}, f32[4,512]{1,0:T(4,128)S(1)}, f32[4,512,512]{2,1,0:T(8,128)}) fusion(pred[512,512]{0,1:T(8,128)(4,1)S(1)} %get-tuple-element.631, pred[512,512]{0,1:T(8,128)(4,1)S(1)} %get-tuple-element.632, bf16[512,4,128]{0,2,1:T(8,128)(2,1)S(1)} %bitcast.121, bf16[4,512,128]{2,1,0:T(8,128)(2,1)S(1)} %get-tuple-element.682), kind=kOutput, calls=%fused_computation.19.clone.1 | convolution fusion | flops 273674240 | bytes 5783552 | tf_op jit(solution)/shard_map/while/body/eval_jaxpr/gqd,tgd->gqt/dot_general | solution.py:17
  123.8 3.7 %fusion.82 = (f32[4,512]{1,0:T(4,128)S(1)}, f32[4,512]{1,0:T(4,128)S(1)}) fusion(f32[4,512,512]{2,1,0:T(8,128)} %get-tuple-element.634, f32[4,512]{1,0:T(4,128)S(1)} %select_maximum_fusion.5, pred[512,512]{0,1:T(8,128)(4,1)S(1)} %get-tuple-element.631, f32[4,512]{1,0:T(4,128)S(1)} %select_maximum_fusion.4, pred[512,512]{0,1:T(8,128)(4,1)S(1)} %get-tuple-element.632), kind=kLoop, calls=%fused_computation.23.clone.1 | loop fusion | flops 9433088 | bytes 4751360 | tf_op jit(solution)/shard_map/while/body/eval_jaxpr/reduce_sum | solution.py:34
  128.6 1.9 fusion.85
  134.0 3.4 %fusion.81 = (f32[4,512]{1,0:T(4,128)S(1)}, f32[4,512]{1,0:T(4,128)S(1)}, f32[4,512,512]{2,1,0:T(8,128)}) fusion(pred[512,512]{0,1:T(8,128)(4,1)S(1)} %get-tuple-element.631, pred[512,512]{0,1:T(8,128)(4,1)S(1)} %get-tuple-element.632, bf16[512,4,128]{0,2,1:T(8,128)(2,1)S(1)} %bitcast.121, bf16[4,512,128]{2,1,0:T(8,128)(2,1)S(1)} %get-tuple-element.682), kind=kOutput, calls=%fused_computation.19.clone.1 | convolution fusion | flops 273674240 | bytes 5783552 | tf_op jit(solution)/shard_map/while/body/eval_jaxpr/gqd,tgd->gqt/dot_general | solution.py:17
  137.4 3.7 %fusion.82 = (f32[4,512]{1,0:T(4,128)S(1)}, f32[4,512]{1,0:T(4,128)S(1)}) fusion(f32[4,512,512]{2,1,0:T(8,128)} %get-tuple-element.634, f32[4,512]{1,0:T(4,128)S(1)} %select_maximum_fusion.5, pred[512,512]{0,1:T(8,128)(4,1)S(1)} %get-tuple-element.631, f32[4,512]{1,0:T(4,128)S(1)} %select_maximum_fusion.4, pred[512,512]{0,1:T(8,128)(4,1)S(1)} %get-tuple-element.632), kind=kLoop, calls=%fused_computation.23.clone.1 | loop fusion | flops 9433088 | bytes 4751360 | tf_op jit(solution)/shard_map/while/body/eval_jaxpr/reduce_sum | solution.py:34
  142.3 1.9 fusion.85
  144.2 1.9 fusion.84
  147.7 3.4 %fusion.81 = (f32[4,512]{1,0:T(4,128)S(1)}, f32[4,512]{1,0:T(4,128)S(1)}, f32[4,512,512]{2,1,0:T(8,128)}) fusion(pred[512,512]{0,1:T(8,128)(4,1)S(1)} %get-tuple-element.631, pred[512,512]{0,1:T(8,128)(4,1)S(1)} %get-tuple-element.632, bf16[512,4,128]{0,2,1:T(8,128)(2,1)S(1)} %bitcast.121, bf16[4,512,128]{2,1,0:T(8,128)(2,1)S(1)} %get-tuple-element.682), kind=kOutput, calls=%fused_computation.19.clone.1 | convolution fusion | flops 273674240 | bytes 5783552 | tf_op jit(solution)/shard_map/while/body/eval_jaxpr/gqd,tgd->gqt/dot_general | solution.py:17
  151.1 3.7 %fusion.82 = (f32[4,512]{1,0:T(4,128)S(1)}, f32[4,512]{1,0:T(4,128)S(1)}) fusion(f32[4,512,512]{2,1,0:T(8,128)} %get-tuple-element.634, f32[4,512]{1,0:T(4,128)S(1)} %select_maximum_fusion.5, pred[512,512]{0,1:T(8,128)(4,1)S(1)} %get-tuple-element.631, f32[4,512]{1,0:T(4,128)S(1)} %select_maximum_fusion.4, pred[512,512]{0,1:T(8,128)(4,1)S(1)} %get-tuple-element.632), kind=kLoop, calls=%fused_computation.23.clone.1 | loop fusion | flops 9433088 | bytes 4751360 | tf_op jit(solution)/shard_map/while/body/eval_jaxpr/reduce_sum | solution.py:34
  155.9 1.9 fusion.85
  159.8 2.1 multiply_reduce_fusion
  162.2 9.5 %fusion.39 = f32[128,4096]{1,0:T(8,128)} fusion(bf16[128,2048]{0,1:T(8,128)(2,1)S(1)} %bitcast.122, bf16[2048,4096]{1,0:T(8,128)(2,1)} %param.15), kind=kOutput, calls=%fused_computation.70 | convolution fusion | flops 2147483648 | bytes 19398656 | tf_op jit(solution)/shard_map/dot_general | solution.py:167
  171.8 18.3 %while.38 = (s32[]{:T(128)}, f32[2048]{0:T(1024)S(1)}, bf16[2048,512]{0,1:T(8,128)(2,1)}, bf16[4,512,128]{2,1,0:T(8,128)(2,1)S(1)}, f32[4,512]{1,0:T(4,128)S(1)}...) while((s32[]{:T(128)}, f32[2048]{0:T(1024)S(1)}, ...), condition=%wide.region_11.12_spmd.clone, body=%wide.region_9.11_spmd.clone.sunk | while | flops 546570752 | bytes 13140663 | solution.py:81
  174.0 2.1 fusion.74
  178.7 2.1 fusion.74
  183.2 2.1 fusion.74
  187.7 2.1 fusion.74
  190.0 9.4 %all-reduce = f32[2048]{0:T(1024)S(1)} all-reduce(f32[2048]{0:T(1024)S(1)} %get-tuple-element.365), channel_id=3, replica_groups=mesh['groups'=2,'ctx'=4,'head'=2,'rep'=2] {'ctx'}, use_global_device_ids=true, to_apply=%region_12.13.clone | all-reduce | flops 2048 | bytes 16384
  199.5 5.6 %psum.14 = f32[512]{0:T(512)S(1)} all-reduce(f32[512]{0:T(512)S(1)} %dynamic-slice.1), channel_id=1, replica_groups=mesh['groups'=2,'ctx'=4,'head'=2,'rep'=2] {'head','rep'}, use_global_device_ids=true, to_apply=%region_13.14 | all-reduce | flops 512 | bytes 4096 | tf_op jit(solution)/shard_map/psum | solution.py:171
  205.4 10.0 %psum.15 = f32[32]{0:T(128)} all-reduce(f32[32]{0:T(128)S(1)} %convolution_bitcast_fusion), channel_id=1, replica_groups=mesh['groups'=2,'ctx'=4,'head'=2,'rep'=2] {'ctx'}, use_global_device_ids=true, to_apply=%region_14.15 | all-reduce | flops 32 | bytes 256 | tf_op jit(solution)/shard_map/psum | solution.py:175
  215.4 2.1 convert_element_type.44
  (136 shorter events, 27.8 us)
Async XLA Ops:
  7.2 6.0 %copy-start.4 = (s32[512]{0:T(512)S(1)}, s32[512]{0:T(512)}, u32[]{:S(2)}) copy-start(s32[512]{0:T(512)} %param.18) | copy-start | bytes 6148
  7.2 6.0 %copy-start.6 = (s32[4]{0:T(128)S(1)}, s32[4]{0:T(128)}, u32[]{:S(2)}) copy-start(s32[4]{0:T(128)} %param.19) | copy-start | bytes 52
  7.2 19.9 %copy-start.7 = (s32[128]{0:T(128)S(1)}, s32[128]{0:T(128)}, u32[]{:S(2)}) copy-start(s32[128]{0:T(128)} %param.17) | copy-start | bytes 1540
  7.2 19.9 %copy-start.3 = (bf16[128,4096]{1,0:T(8,128)(2,1)S(1)}, bf16[128,4096]{1,0:T(8,128)(2,1)}, u32[]{:S(2)}) copy-start(bf16[128,4096]{1,0:T(8,128)(2,1)} %param.16) | copy-start | bytes 3145732
  7.2 51.7 %all-gather.4.cloned.1.call-start = ((), (), s32[]{:S(2)}) async-start(), calls=%async_computation.1 | async-start | bytes 2621440 | tf_op jit(solution)/shard_map/all_gather | solution.py:132
  9.4 95.8 %all-gather.6.cloned.1.call-start = ((), (), s32[]{:S(2)}) async-start(), calls=%async_computation.2 | async-start | bytes 2621440 | tf_op jit(solution)/shard_map/all_gather | solution.py:133
  11.5 203.9 %reduce-scatter.2.cloned.1.call-start = ((), (), s32[]{:S(2)}) async-start(), calls=%async_computation.3 | async-start | bytes 3145728 | tf_op jit(solution)/shard_map/reduce_scatter | solution.py:168
  27.1 12.1 %copy-start.8 = (u32[32]{0:T(128)S(1)}, u32[32]{0:T(128)}, u32[]{:S(2)}) copy-start(u32[32]{0:T(128)} %constant.131) | copy-start | bytes 388
  110.1 4.9 %copy-start = (f32[4,512,512]{2,1,0:T(8,128)S(1)}, f32[4,512,512]{2,1,0:T(8,128)}, u32[]{:S(2)}) copy-start(f32[4,512,512]{2,1,0:T(8,128)} %get-tuple-element.634) | copy-start | bytes 12582916 | tf_op jit(solution)/shard_map/while
  110.1 4.9 %copy-start.1 = (f32[4,512,128]{2,1,0:T(8,128)S(1)}, f32[4,512,128]{2,1,0:T(8,128)}, u32[]{:S(2)}) copy-start(f32[4,512,128]{2,1,0:T(8,128)} %get-tuple-element.664) | copy-start | bytes 3145732 | tf_op jit(solution)/shard_map/while
  116.9 1.9 copy-start.2
  123.8 4.9 %copy-start = (f32[4,512,512]{2,1,0:T(8,128)S(1)}, f32[4,512,512]{2,1,0:T(8,128)}, u32[]{:S(2)}) copy-start(f32[4,512,512]{2,1,0:T(8,128)} %get-tuple-element.634) | copy-start | bytes 12582916 | tf_op jit(solution)/shard_map/while
  123.8 4.9 %copy-start.1 = (f32[4,512,128]{2,1,0:T(8,128)S(1)}, f32[4,512,128]{2,1,0:T(8,128)}, u32[]{:S(2)}) copy-start(f32[4,512,128]{2,1,0:T(8,128)} %get-tuple-element.664) | copy-start | bytes 3145732 | tf_op jit(solution)/shard_map/while
  130.6 1.9 copy-start.2
  137.4 4.9 %copy-start = (f32[4,512,512]{2,1,0:T(8,128)S(1)}, f32[4,512,512]{2,1,0:T(8,128)}, u32[]{:S(2)}) copy-start(f32[4,512,512]{2,1,0:T(8,128)} %get-tuple-element.634) | copy-start | bytes 12582916 | tf_op jit(solution)/shard_map/while
  137.4 4.9 %copy-start.1 = (f32[4,512,128]{2,1,0:T(8,128)S(1)}, f32[4,512,128]{2,1,0:T(8,128)}, u32[]{:S(2)}) copy-start(f32[4,512,128]{2,1,0:T(8,128)} %get-tuple-element.664) | copy-start | bytes 3145732 | tf_op jit(solution)/shard_map/while
  144.2 1.9 copy-start.2
  151.0 4.9 %copy-start = (f32[4,512,512]{2,1,0:T(8,128)S(1)}, f32[4,512,512]{2,1,0:T(8,128)}, u32[]{:S(2)}) copy-start(f32[4,512,512]{2,1,0:T(8,128)} %get-tuple-element.634) | copy-start | bytes 12582916 | tf_op jit(solution)/shard_map/while
  151.0 4.9 %copy-start.1 = (f32[4,512,128]{2,1,0:T(8,128)S(1)}, f32[4,512,128]{2,1,0:T(8,128)}, u32[]{:S(2)}) copy-start(f32[4,512,128]{2,1,0:T(8,128)} %get-tuple-element.664) | copy-start | bytes 3145732 | tf_op jit(solution)/shard_map/while
  157.8 1.9 copy-start.2
  205.1 12.4 %copy-start.5 = (f32[512]{0:T(512)}, f32[512]{0:T(512)S(1)}, u32[]{:S(2)}) copy-start(f32[512]{0:T(512)S(1)} %psum.14) | copy-start | bytes 6148
Sparse Core Ops, SparseCore 0:
  10.2 48.6 all-gather.3
  60.4 44.7 all-gather.5
  171.9 30.5 reduce-scatter.1
where the time goes:
time: 225 us; the launch traced here: 224 us
  waiting for transfers between devices  64.7 us (29%)
  matrix products  61.2 us (27%)
  blocking collectives  38.7 us (17%)
  other arithmetic  22.6 us (10%)
  local copies, waits for them, and re-layouts  21.4 us (10%)
  between operations  14.7 us (7%)
    all_gather x1, waiting for transfers between devices, local(): lax.all_gather(value, 'ctx', axis=0, tiled=True)  46.4 us
    all_gather x1, waiting for transfers between devices, local(): lax.all_gather(key, 'ctx', axis=0, tiled=True)  18.3 us
    dot_general x8, matrix products, block_scores(): jnp.einsum('gqd,tgd->gqt', query_rows, split_heads(key_block), preferred_...  16.3 us
    dot_general x8, matrix products, online_update(): jnp.einsum('gqt,tgd->gqd', weights.astype(jnp.bfloat16), value_heads, pre...  15.3 us
    reduce_sum x4, other arithmetic, online_update(): row_total = row_total * shrink + jnp.sum(weights, axis=2)  14.8 us
    dynamic_slice x12, local copies, waits for them, and re-layouts, advance(): lax.dynamic_slice_in_dim(member, offset, block_rows, 0)  14 us
    all_gather x1, blocking collectives, local(): lax.all_gather(kept_flag, 'ctx', axis=0, tiled=True)  13.7 us
    dot_general x1, matrix products, local(): jnp.dot(grad_masked, out_weight.T, preferred_element_type=jnp.float32)  11.5 us
  transfers between devices with their start and end apart: 3, of which 2 were waited for; matrix products, arithmetic and copies ran while one was open for 16% of the time, Pallas kernels for 0%

commit v1 on v0

--- a/solution.py
+++ b/solution.py
@@ -168,7 +168,7 @@
     patch_effect = lax.psum_scatter(projected, "head", scatter_dimension=1, tiled=True).astype(
         jnp.bfloat16
     )
-    token_attr = lax.psum(local_attr, ("head", "rep"))
+    token_attr = lax.psum(lax.psum(local_attr, "rep"), "head")
     onehot = (
         segment_ids[:, None] == jnp.arange(SEG_DEV * ctx_count, dtype=jnp.int32)[None, :]
     ).astype(jnp.float32)

time: 225 us -> 227 us (level)
    psum x1 -> x2, blocking collectives: 5.63 us -> 7.36 us  [local(): token_attr = lax.psum(lax.psum(local_attr, 'rep'), 'head')]
  transfers between devices with their start and end apart: 3 -> 3, of which waited for: 2 -> 2; matrix products, arithmetic and copies ran while one was open for 16% -> 15% of each run, Pallas kernels for 0% -> 0%
where the time goes in v1:
time: 227 us; the launch traced here: 226 us
  waiting for transfers between devices  64.7 us (29%)
  matrix products  61.3 us (27%)
  blocking collectives  40.4 us (18%)
  other arithmetic  22.6 us (10%)
  local copies, waits for them, and re-layouts  21.4 us (9%)
  between operations  14.7 us (6%)
    all_gather x1, waiting for transfers between devices, local(): lax.all_gather(value, 'ctx', axis=0, tiled=True)  46.4 us
    all_gather x1, waiting for transfers between devices, local(): lax.all_gather(key, 'ctx', axis=0, tiled=True)  18.3 us
    dot_general x8, matrix products, block_scores(): jnp.einsum('gqd,tgd->gqt', query_rows, split_heads(key_block), preferred_...  16.3 us
    dot_general x8, matrix products, online_update(): jnp.einsum('gqt,tgd->gqd', weights.astype(jnp.bfloat16), value_heads, pre...  15.3 us
    reduce_sum x4, other arithmetic, online_update(): row_total = row_total * shrink + jnp.sum(weights, axis=2)  14.8 us
    dynamic_slice x12, local copies, waits for them, and re-layouts, advance(): lax.dynamic_slice_in_dim(member, offset, block_rows, 0)  14 us
    all_gather x1, blocking collectives, local(): lax.all_gather(kept_flag, 'ctx', axis=0, tiled=True)  13.7 us
    dot_general x1, matrix products, local(): jnp.dot(grad_masked, out_weight.T, preferred_element_type=jnp.float32)  11.5 us
  transfers between devices with their start and end apart: 3, of which 2 were waited for; matrix products, arithmetic and copies ran while one was open for 15% of the time, Pallas kernels for 0%

profile of v1, /device:TPU:0, one launch (start us, length us, event | category | flops | bytes accessed | tf_op | source)
XLA Modules:
  0.0 225.8 jit_solution(934154797035908858)
XLA Ops:
  7.3 2.1 copy.57
  9.5 2.0 copy.59
  13.3 13.7 %all-gather = bf16[4,1,512]{2,1,0:T(2,128)(2,1)S(1)} all-gather(bf16[1,1,512]{2,1,0:T(2,128)(2,1)S(1)} %reshape.205), channel_id=1, replica_groups=mesh['groups'=2,'ctx'=4,'head'=2,'rep'=2] {'ctx'}, dimensions={0}, use_global_device_ids=true | all-gather | bytes 5120 | tf_op jit(solution)/shard_map/all_gather | solution.py:134
  27.1 11.5 %convolution_convert_fusion = bf16[128,2048]{1,0:T(8,128)(2,1)S(1)} fusion(bf16[2048,4096]{1,0:T(8,128)(2,1)} %param.15, bf16[128,4096]{1,0:T(8,128)(2,1)S(1)} %copy-done.3, pred[128]{0:T(512)(128)(4,1)S(1)} %broadcast_compare_fusion.2), kind=kOutput, calls=%fused_computation.53 | convolution fusion | flops 2148270080 | bytes 18350208 | tf_op jit(solution)/shard_map/dot_general | solution.py:106
  40.5 18.3 %all-gather.4.cloned.1.call-done = bf16[2048,512]{0,1:T(8,128)(2,1)} async-done(((bf16[512,512]{0,1:T(8,128)(2,1)}), bf16[2048,512]{0,1:T(8,128)(2,1)}) %all-gather.4.cloned.1.call-update) | async-done | bytes 2097168 | tf_op jit(solution)/shard_map/all_gather | solution.py:132
  58.9 46.4 %all-gather.6.cloned.1.call-done = bf16[2048,512]{0,1:T(8,128)(2,1)} async-done(((bf16[512,512]{0,1:T(8,128)(2,1)}), bf16[2048,512]{0,1:T(8,128)(2,1)}) %all-gather.6.cloned.1.call-update) | async-done | bytes 2097168 | tf_op jit(solution)/shard_map/all_gather | solution.py:133
  105.2 54.5 %while.39 = (s32[]{:T(128)}, f32[4,512]{1,0:T(4,128)S(1)}, f32[4,512]{1,0:T(4,128)S(1)}, f32[4,512,128]{2,1,0:T(8,128)S(1)}, f32[4,512]{1,0:T(4,128)S(1)}, /*ind...) while((s32[]{:T(128)}, f32[4,512]{1,0:T(4,128)S(1)}, ...), condition=%wide.region_6.7_spmd.clone, body=%wide.region_1.6_spmd.clone.sunk | while | flops 832591872 | bytes 52702004 | solution.py:81
  106.7 3.4 %fusion.81 = (f32[4,512]{1,0:T(4,128)S(1)}, f32[4,512]{1,0:T(4,128)S(1)}, f32[4,512,512]{2,1,0:T(8,128)}) fusion(pred[512,512]{0,1:T(8,128)(4,1)S(1)} %get-tuple-element.631, pred[512,512]{0,1:T(8,128)(4,1)S(1)} %get-tuple-element.632, bf16[512,4,128]{0,2,1:T(8,128)(2,1)S(1)} %bitcast.121, bf16[4,512,128]{2,1,0:T(8,128)(2,1)S(1)} %get-tuple-element.682), kind=kOutput, calls=%fused_computation.19.clone.1 | convolution fusion | flops 273674240 | bytes 5783552 | tf_op jit(solution)/shard_map/while/body/eval_jaxpr/gqd,tgd->gqt/dot_general | solution.py:17
  110.1 3.7 %fusion.82 = (f32[4,512]{1,0:T(4,128)S(1)}, f32[4,512]{1,0:T(4,128)S(1)}) fusion(f32[4,512,512]{2,1,0:T(8,128)} %get-tuple-element.634, f32[4,512]{1,0:T(4,128)S(1)} %select_maximum_fusion.5, pred[512,512]{0,1:T(8,128)(4,1)S(1)} %get-tuple-element.631, f32[4,512]{1,0:T(4,128)S(1)} %select_maximum_fusion.4, pred[512,512]{0,1:T(8,128)(4,1)S(1)} %get-tuple-element.632), kind=kLoop, calls=%fused_computation.23.clone.1 | loop fusion | flops 9433088 | bytes 4751360 | tf_op jit(solution)/shard_map/while/body/eval_jaxpr/reduce_sum | solution.py:34
  115.0 1.9 fusion.85
  116.9 1.9 fusion.84
  120.4 3.4 %fusion.81 = (f32[4,512]{1,0:T(4,128)S(1)}, f32[4,512]{1,0:T(4,128)S(1)}, f32[4,512,512]{2,1,0:T(8,128)}) fusion(pred[512,512]{0,1:T(8,128)(4,1)S(1)} %get-tuple-element.631, pred[512,512]{0,1:T(8,128)(4,1)S(1)} %get-tuple-element.632, bf16[512,4,128]{0,2,1:T(8,128)(2,1)S(1)} %bitcast.121, bf16[4,512,128]{2,1,0:T(8,128)(2,1)S(1)} %get-tuple-element.682), kind=kOutput, calls=%fused_computation.19.clone.1 | convolution fusion | flops 273674240 | bytes 5783552 | tf_op jit(solution)/shard_map/while/body/eval_jaxpr/gqd,tgd->gqt/dot_general | solution.py:17
  123.8 3.7 %fusion.82 = (f32[4,512]{1,0:T(4,128)S(1)}, f32[4,512]{1,0:T(4,128)S(1)}) fusion(f32[4,512,512]{2,1,0:T(8,128)} %get-tuple-element.634, f32[4,512]{1,0:T(4,128)S(1)} %select_maximum_fusion.5, pred[512,512]{0,1:T(8,128)(4,1)S(1)} %get-tuple-element.631, f32[4,512]{1,0:T(4,128)S(1)} %select_maximum_fusion.4, pred[512,512]{0,1:T(8,128)(4,1)S(1)} %get-tuple-element.632), kind=kLoop, calls=%fused_computation.23.clone.1 | loop fusion | flops 9433088 | bytes 4751360 | tf_op jit(solution)/shard_map/while/body/eval_jaxpr/reduce_sum | solution.py:34
  128.6 1.9 fusion.85
  134.0 3.4 %fusion.81 = (f32[4,512]{1,0:T(4,128)S(1)}, f32[4,512]{1,0:T(4,128)S(1)}, f32[4,512,512]{2,1,0:T(8,128)}) fusion(pred[512,512]{0,1:T(8,128)(4,1)S(1)} %get-tuple-element.631, pred[512,512]{0,1:T(8,128)(4,1)S(1)} %get-tuple-element.632, bf16[512,4,128]{0,2,1:T(8,128)(2,1)S(1)} %bitcast.121, bf16[4,512,128]{2,1,0:T(8,128)(2,1)S(1)} %get-tuple-element.682), kind=kOutput, calls=%fused_computation.19.clone.1 | convolution fusion | flops 273674240 | bytes 5783552 | tf_op jit(solution)/shard_map/while/body/eval_jaxpr/gqd,tgd->gqt/dot_general | solution.py:17
  137.4 3.7 %fusion.82 = (f32[4,512]{1,0:T(4,128)S(1)}, f32[4,512]{1,0:T(4,128)S(1)}) fusion(f32[4,512,512]{2,1,0:T(8,128)} %get-tuple-element.634, f32[4,512]{1,0:T(4,128)S(1)} %select_maximum_fusion.5, pred[512,512]{0,1:T(8,128)(4,1)S(1)} %get-tuple-element.631, f32[4,512]{1,0:T(4,128)S(1)} %select_maximum_fusion.4, pred[512,512]{0,1:T(8,128)(4,1)S(1)} %get-tuple-element.632), kind=kLoop, calls=%fused_computation.23.clone.1 | loop fusion | flops 9433088 | bytes 4751360 | tf_op jit(solution)/shard_map/while/body/eval_jaxpr/reduce_sum | solution.py:34
  142.3 1.9 fusion.85
  147.7 3.4 %fusion.81 = (f32[4,512]{1,0:T(4,128)S(1)}, f32[4,512]{1,0:T(4,128)S(1)}, f32[4,512,512]{2,1,0:T(8,128)}) fusion(pred[512,512]{0,1:T(8,128)(4,1)S(1)} %get-tuple-element.631, pred[512,512]{0,1:T(8,128)(4,1)S(1)} %get-tuple-element.632, bf16[512,4,128]{0,2,1:T(8,128)(2,1)S(1)} %bitcast.121, bf16[4,512,128]{2,1,0:T(8,128)(2,1)S(1)} %get-tuple-element.682), kind=kOutput, calls=%fused_computation.19.clone.1 | convolution fusion | flops 273674240 | bytes 5783552 | tf_op jit(solution)/shard_map/while/body/eval_jaxpr/gqd,tgd->gqt/dot_general | solution.py:17
  151.1 3.7 %fusion.82 = (f32[4,512]{1,0:T(4,128)S(1)}, f32[4,512]{1,0:T(4,128)S(1)}) fusion(f32[4,512,512]{2,1,0:T(8,128)} %get-tuple-element.634, f32[4,512]{1,0:T(4,128)S(1)} %select_maximum_fusion.5, pred[512,512]{0,1:T(8,128)(4,1)S(1)} %get-tuple-element.631, f32[4,512]{1,0:T(4,128)S(1)} %select_maximum_fusion.4, pred[512,512]{0,1:T(8,128)(4,1)S(1)} %get-tuple-element.632), kind=kLoop, calls=%fused_computation.23.clone.1 | loop fusion | flops 9433088 | bytes 4751360 | tf_op jit(solution)/shard_map/while/body/eval_jaxpr/reduce_sum | solution.py:34
  155.9 1.9 fusion.85
  159.8 2.1 multiply_reduce_fusion
  162.2 9.5 %fusion.39 = f32[128,4096]{1,0:T(8,128)} fusion(bf16[128,2048]{0,1:T(8,128)(2,1)S(1)} %bitcast.122, bf16[2048,4096]{1,0:T(8,128)(2,1)} %param.15), kind=kOutput, calls=%fused_computation.70 | convolution fusion | flops 2147483648 | bytes 19398656 | tf_op jit(solution)/shard_map/dot_general | solution.py:167
  171.8 18.3 %while.38 = (s32[]{:T(128)}, f32[2048]{0:T(1024)S(1)}, bf16[2048,512]{0,1:T(8,128)(2,1)}, bf16[4,512,128]{2,1,0:T(8,128)(2,1)S(1)}, f32[4,512]{1,0:T(4,128)S(1)}...) while((s32[]{:T(128)}, f32[2048]{0:T(1024)S(1)}, ...), condition=%wide.region_11.12_spmd.clone, body=%wide.region_9.11_spmd.clone.sunk | while | flops 546570752 | bytes 13140663 | solution.py:81
  174.0 2.1 fusion.74
  178.7 2.1 fusion.74
  183.3 2.1 fusion.74
  187.8 2.1 fusion.74
  190.1 9.4 %all-reduce = f32[2048]{0:T(1024)S(1)} all-reduce(f32[2048]{0:T(1024)S(1)} %get-tuple-element.365), channel_id=3, replica_groups=mesh['groups'=2,'ctx'=4,'head'=2,'rep'=2] {'ctx'}, use_global_device_ids=true, to_apply=%region_12.13.clone | all-reduce | flops 2048 | bytes 16384
  199.6 2.4 %psum.21 = f32[512]{0:T(512)S(1)} all-reduce(f32[512]{0:T(512)S(1)} %dynamic-slice.1), channel_id=1, replica_groups=mesh['groups'=2,'ctx'=4,'head'=2,'rep'=2] {'rep'}, use_global_device_ids=true, to_apply=%region_13.14 | all-reduce | flops 512 | bytes 4096 | tf_op jit(solution)/shard_map/psum | solution.py:171
  202.0 4.9 %psum.22 = f32[512]{0:T(512)S(1)} all-reduce(f32[512]{0:T(512)S(1)} %psum.21), channel_id=1, replica_groups=mesh['groups'=2,'ctx'=4,'head'=2,'rep'=2] {'head'}, use_global_device_ids=true, to_apply=%region_14.15 | all-reduce | flops 512 | bytes 4096 | tf_op jit(solution)/shard_map/psum | solution.py:171
  207.2 10.0 %psum.23 = f32[32]{0:T(128)} all-reduce(f32[32]{0:T(128)S(1)} %convolution_bitcast_fusion), channel_id=1, replica_groups=mesh['groups'=2,'ctx'=4,'head'=2,'rep'=2] {'ctx'}, use_global_device_ids=true, to_apply=%region_15.16 | all-reduce | flops 32 | bytes 256 | tf_op jit(solution)/shard_map/psum | solution.py:175
  217.2 2.1 convert_element_type.44
  (137 shorter events, 29.7 us)
Async XLA Ops:
  7.2 6.0 %copy-start.4 = (s32[512]{0:T(512)S(1)}, s32[512]{0:T(512)}, u32[]{:S(2)}) copy-start(s32[512]{0:T(512)} %param.18) | copy-start | bytes 6148
  7.2 6.0 %copy-start.6 = (s32[4]{0:T(128)S(1)}, s32[4]{0:T(128)}, u32[]{:S(2)}) copy-start(s32[4]{0:T(128)} %param.19) | copy-start | bytes 52
  7.2 19.9 %copy-start.7 = (s32[128]{0:T(128)S(1)}, s32[128]{0:T(128)}, u32[]{:S(2)}) copy-start(s32[128]{0:T(128)} %param.17) | copy-start | bytes 1540
  7.2 19.9 %copy-start.3 = (bf16[128,4096]{1,0:T(8,128)(2,1)S(1)}, bf16[128,4096]{1,0:T(8,128)(2,1)}, u32[]{:S(2)}) copy-start(bf16[128,4096]{1,0:T(8,128)(2,1)} %param.16) | copy-start | bytes 3145732
  7.2 51.7 %all-gather.4.cloned.1.call-start = ((), (), s32[]{:S(2)}) async-start(), calls=%async_computation.1 | async-start | bytes 2621440 | tf_op jit(solution)/shard_map/all_gather | solution.py:132
  9.4 95.8 %all-gather.6.cloned.1.call-start = ((), (), s32[]{:S(2)}) async-start(), calls=%async_computation.2 | async-start | bytes 2621440 | tf_op jit(solution)/shard_map/all_gather | solution.py:133
  11.5 205.7 %reduce-scatter.2.cloned.1.call-start = ((), (), s32[]{:S(2)}) async-start(), calls=%async_computation.3 | async-start | bytes 3145728 | tf_op jit(solution)/shard_map/reduce_scatter | solution.py:168
  27.1 12.1 %copy-start.8 = (u32[32]{0:T(128)S(1)}, u32[32]{0:T(128)}, u32[]{:S(2)}) copy-start(u32[32]{0:T(128)} %constant.131) | copy-start | bytes 388
  110.1 4.9 %copy-start = (f32[4,512,512]{2,1,0:T(8,128)S(1)}, f32[4,512,512]{2,1,0:T(8,128)}, u32[]{:S(2)}) copy-start(f32[4,512,512]{2,1,0:T(8,128)} %get-tuple-element.634) | copy-start | bytes 12582916 | tf_op jit(solution)/shard_map/while
  110.1 4.9 %copy-start.1 = (f32[4,512,128]{2,1,0:T(8,128)S(1)}, f32[4,512,128]{2,1,0:T(8,128)}, u32[]{:S(2)}) copy-start(f32[4,512,128]{2,1,0:T(8,128)} %get-tuple-element.664) | copy-start | bytes 3145732 | tf_op jit(solution)/shard_map/while
  116.9 1.9 copy-start.2
  123.8 4.9 %copy-start = (f32[4,512,512]{2,1,0:T(8,128)S(1)}, f32[4,512,512]{2,1,0:T(8,128)}, u32[]{:S(2)}) copy-start(f32[4,512,512]{2,1,0:T(8,128)} %get-tuple-element.634) | copy-start | bytes 12582916 | tf_op jit(solution)/shard_map/while
  123.8 4.9 %copy-start.1 = (f32[4,512,128]{2,1,0:T(8,128)S(1)}, f32[4,512,128]{2,1,0:T(8,128)}, u32[]{:S(2)}) copy-start(f32[4,512,128]{2,1,0:T(8,128)} %get-tuple-element.664) | copy-start | bytes 3145732 | tf_op jit(solution)/shard_map/while
  130.6 1.9 copy-start.2
  137.4 4.9 %copy-start = (f32[4,512,512]{2,1,0:T(8,128)S(1)}, f32[4,512,512]{2,1,0:T(8,128)}, u32[]{:S(2)}) copy-start(f32[4,512,512]{2,1,0:T(8,128)} %get-tuple-element.634) | copy-start | bytes 12582916 | tf_op jit(solution)/shard_map/while
  137.4 4.9 %copy-start.1 = (f32[4,512,128]{2,1,0:T(8,128)S(1)}, f32[4,512,128]{2,1,0:T(8,128)}, u32[]{:S(2)}) copy-start(f32[4,512,128]{2,1,0:T(8,128)} %get-tuple-element.664) | copy-start | bytes 3145732 | tf_op jit(solution)/shard_map/while
  144.2 1.9 copy-start.2
  151.0 4.9 %copy-start = (f32[4,512,512]{2,1,0:T(8,128)S(1)}, f32[4,512,512]{2,1,0:T(8,128)}, u32[]{:S(2)}) copy-start(f32[4,512,512]{2,1,0:T(8,128)} %get-tuple-element.634) | copy-start | bytes 12582916 | tf_op jit(solution)/shard_map/while
  151.0 4.9 %copy-start.1 = (f32[4,512,128]{2,1,0:T(8,128)S(1)}, f32[4,512,128]{2,1,0:T(8,128)}, u32[]{:S(2)}) copy-start(f32[4,512,128]{2,1,0:T(8,128)} %get-tuple-element.664) | copy-start | bytes 3145732 | tf_op jit(solution)/shard_map/while
  157.8 1.9 copy-start.2
  206.9 12.3 %copy-start.5 = (f32[512]{0:T(512)}, f32[512]{0:T(512)S(1)}, u32[]{:S(2)}) copy-start(f32[512]{0:T(512)S(1)} %psum.22) | copy-start | bytes 6148
Sparse Core Ops, SparseCore 0:
  10.2 48.6 all-gather.3
  60.4 44.7 all-gather.5
  171.9 30.5 reduce-scatter.1
